TPU v7x, 32 devices: a whole 2x2x4 slice. The times are simulated.
32 devices in a mesh: groups: 2 (over y), sec: 4 (over x, core), plane: 4 (over z).
Axes of the slice: x: 2, y: 2, z: 4, core: 2. Of those that a mesh axis runs over, the one named last changes fastest.
Arguments:
- tokens: bfloat16 [16, 512, 1024], P(('groups', 'sec'), 'plane'), parts along dimension 0, may hold values from -8 to 8
- counts: int32 [16], P('groups'), parts along dimension 0, may hold values from 128 to 512, as said below
- region_ids: int32 [16, 512], P(('groups', 'sec'), 'plane'), parts along dimension 0, may hold values from 0 to 31
- norm_gains: float32 [2, 1024], replicated, may hold values from 0.1 to 1.9
- cross_qkv: bfloat16 [1024, 3072], P('plane'), may hold values from -2 to 2
- cross_out: bfloat16 [1024, 1024], P('plane'), may hold values from -0.1875 to 0.1875
- plane_qkv: bfloat16 [1024, 3072], P('plane'), may hold values from -2 to 2
- plane_out: bfloat16 [1024, 1024], P('plane'), may hold values from -0.1875 to 0.1875
Outputs:
- encoded: bfloat16 [16, 512, 1024], P(('groups', 'sec'), 'plane'), parts along dimension 0
- pooled: float32 [64, 1024], P(('groups', 'sec', 'plane')), parts along dimension 0
There are 2 independent parts, one for each index of `groups`. A program takes and returns all parts, laid end to end along the dimension named above; an argument that names none is the same for every part. Nothing has to cross between parts.
Inputs may be any that keep to these rules, and one draw needn't show every extreme that they name: `counts`: valid tissue tokens of each section; they are the first positions of the section.
All inputs are finite; a program needn't handle non-finite values.
Results may differ from a plain program's by a relative error of at most 0.009.
Values may be sent and summed in bfloat16 or wider, within the bound.
No kernel may reach another device: no remote copies, remote signals or barrier semaphores. Data moves between devices by JAX's collectives and lax.ppermute only.
A program may use at most 64 MiB of HBM per device.

v0:
```python
import math
import jax
import jax.numpy as jnp
from jax import lax
from jax.sharding import PartitionSpec as P

HEADS = 16
HEAD_DIM = 64
WINDOW = 128
negative_big = -1e30


def shifted_2(value, axis, by):
    peers = lax.axis_size(axis)
    pairs = [(i, i + by) for i in range(peers) if 0 <= i + by < peers]
    return lax.ppermute(value, axis, pairs)


def rms_norm(values, gain):
    wide = values.astype(jnp.float32)
    scaled = wide * lax.rsqrt(jnp.mean(wide * wide, axis=-1, keepdims=True) + 1e-06) * gain
    return scaled.astype(jnp.bfloat16)


def masked_softmax(scores, allowed):
    shifted = jnp.where(allowed, scores, negative_big)
    top = jnp.max(shifted, axis=-1, keepdims=True)
    expo = jnp.where(allowed, jnp.exp(shifted - top), 0.0)
    return (expo / jnp.sum(expo, axis=-1, keepdims=True)).astype(jnp.bfloat16)


def fold_product(inputs, weight_piece):
    return jnp.dot(inputs, weight_piece, preferred_element_type=jnp.float32)


def gather_pieces(shard):
    groups = lax.axis_size("groups")
    sections = lax.axis_size("sec")
    pair = 2 if sections % 2 == 0 else 1
    width = shard.shape[1] // (groups * pair)
    g = lax.axis_index("groups")
    k = lax.axis_index("sec") % pair
    own = g * pair + k
    mine = lax.dynamic_slice_in_dim(shard, own * width, width, axis=1)
    first = lax.all_gather(mine, "plane", axis=0, tiled=True)
    by_group = [(own, first)]
    for step in range(1, groups):
        moved = [(i, (i + step) % groups) for i in range(groups)]
        source = lax.rem(g - step + groups, groups)
        by_group.append((source * pair + k, lax.ppermute(first, "groups", moved)))
    held = list(by_group)
    if pair == 2:
        swap = [(i, i ^ 1) for i in range(sections)]
        for piece, block in by_group:
            held.append((piece - k + (1 - k), lax.ppermute(block, "sec", swap)))
    return (held, width)


def project(inputs, pieces):
    held, width = pieces
    out = jnp.zeros((inputs.shape[0], width * len(held)), jnp.float32)
    for piece, block in held:
        part = jnp.dot(inputs, block, preferred_element_type=jnp.float32)
        out = lax.dynamic_update_slice_in_dim(out, part, piece * width, axis=1)
    return out


def attend_items(pieces):
    packed_all, flags_all = pieces
    seq_len = packed_all.shape[2]
    block_len = 512
    score_scale = 1.0 / math.sqrt(HEAD_DIM)
    key_index = jnp.arange(seq_len, dtype=jnp.int32)

    def one_item(item_pair):
        packed, key_flag = item_pair
        key_rows = packed[:, HEAD_DIM : 2 * HEAD_DIM]
        value_rows = packed[:, 2 * HEAD_DIM :]
        key_alive = key_flag > 0.5
        query_blocks = packed[:, :HEAD_DIM].reshape(seq_len // block_len, block_len, HEAD_DIM)
        block_starts = jnp.arange(seq_len // block_len, dtype=jnp.int32) * block_len

        def one_block(block_pair):
            query_rows, offset = block_pair
            scores = (
                jnp.einsum("qd,kd->qk", query_rows, key_rows, preferred_element_type=jnp.float32)
                * score_scale
            )
            own_index = offset + jnp.arange(block_len, dtype=jnp.int32)
            allowed = key_alive[None, :] | (key_index[None, :] == own_index[:, None])
            attention = masked_softmax(scores, allowed)
            return jnp.dot(attention, value_rows, preferred_element_type=jnp.float32).astype(
                jnp.bfloat16
            )

        return lax.map(one_block, (query_blocks, block_starts)).reshape(seq_len, HEAD_DIM)

    return lax.map(one_item, (packed_all[0], flags_all[0]))[None]


def body(tokens, counts, region_ids, norm_gains, cross_qkv, cross_out, plane_qkv, plane_out):
    sec_block, tok_block, model_width = tokens.shape
    plane_count = lax.axis_size("plane")
    regions = 2 * lax.axis_size("sec") * plane_count
    positions = lax.axis_index("plane") * tok_block + jnp.arange(tok_block, dtype=jnp.int32)
    padded_counts = jnp.concatenate(
        [jnp.zeros((1,), jnp.int32), counts, jnp.zeros((1,), jnp.int32)]
    )
    near_counts = lax.dynamic_slice_in_dim(
        padded_counts, lax.axis_index("sec") * sec_block, sec_block + 2
    )
    near_valid = positions[None, :] < near_counts[:, None]
    own_valid = near_valid[1 : sec_block + 1]
    score_scale = 1.0 / math.sqrt(HEAD_DIM)
    cross_qkv_pieces = gather_pieces(cross_qkv)
    cross_out_pieces = gather_pieces(cross_out)
    plane_qkv_pieces = gather_pieces(plane_qkv)
    plane_out_pieces = gather_pieces(plane_out)
    normed = rms_norm(tokens, norm_gains[0])
    inputs = normed.reshape(-1, model_width)
    result = project(inputs, cross_qkv_pieces)
    projected = result.astype(jnp.bfloat16).reshape(sec_block, tok_block, 3 * model_width)
    own_kv = projected[:, :, model_width:]
    from_below = shifted_2(own_kv[sec_block - 1], "sec", 1)
    from_above = shifted_2(own_kv[0], "sec", -1)
    near_kv = jnp.concatenate([from_below[None], own_kv, from_above[None]], axis=0)
    queries = projected[:, :, :model_width]
    windows = tok_block // WINDOW
    query_win = queries.reshape(sec_block, windows, WINDOW, HEADS, HEAD_DIM)
    pair_win = near_kv.reshape(sec_block + 2, windows, WINDOW, 2, HEADS, HEAD_DIM)
    stacked = jnp.concatenate(
        [pair_win[0:sec_block], pair_win[1 : sec_block + 1], pair_win[2 : sec_block + 2]], axis=2
    )
    valid_win = near_valid.reshape(sec_block + 2, windows, WINDOW)
    valid_three = jnp.concatenate(
        [valid_win[0:sec_block], valid_win[1 : sec_block + 1], valid_win[2 : sec_block + 2]], axis=2
    )
    itself = jnp.arange(3 * WINDOW)[None, :] == jnp.arange(WINDOW)[:, None] + WINDOW
    scores = (
        jnp.einsum(
            "snqhd,snkhd->snhqk", query_win, stacked[:, :, :, 0], preferred_element_type=jnp.float32
        )
        * score_scale
    )
    allowed = valid_three[:, :, None, None, :] | itself[None, None, None]
    attention = masked_softmax(scores, allowed)
    context = jnp.einsum(
        "snhqk,snkhd->snqhd", attention, stacked[:, :, :, 1], preferred_element_type=jnp.float32
    )
    context = context.astype(jnp.bfloat16).reshape(-1, model_width)
    result = project(context, cross_out_pieces)
    after_cross = (tokens.reshape(-1, model_width).astype(jnp.float32) + result).astype(
        jnp.bfloat16
    )
    normed = rms_norm(after_cross, norm_gains[1])
    result = project(normed, plane_qkv_pieces)
    projected = result.astype(jnp.bfloat16).reshape(sec_block, tok_block, 3, HEADS, HEAD_DIM)
    per_device = sec_block * HEADS // plane_count
    heads_first = jnp.transpose(projected, (0, 3, 1, 2, 4)).reshape(
        plane_count, per_device, tok_block, 3 * HEAD_DIM
    )
    key_flags = jnp.broadcast_to(own_valid[:, None, :], (sec_block, HEADS, tok_block)).astype(
        jnp.bfloat16
    )
    key_flags = key_flags.reshape(plane_count, per_device, tok_block)
    attended = attend_items(
        (
            lax.all_to_all(heads_first, "plane", split_axis=0, concat_axis=2, tiled=True),
            lax.all_to_all(key_flags, "plane", split_axis=0, concat_axis=2, tiled=True),
        )
    )
    returned = lax.all_to_all(attended, "plane", split_axis=2, concat_axis=0, tiled=True)
    context = jnp.transpose(
        returned.reshape(sec_block, HEADS, tok_block, HEAD_DIM), (0, 2, 1, 3)
    ).reshape(-1, model_width)
    result = project(context, plane_out_pieces)
    encoded = (after_cross.astype(jnp.float32) + result).astype(jnp.bfloat16)
    labels = region_ids.reshape(-1)
    member = (jnp.arange(regions, dtype=jnp.int32)[:, None] == labels[None, :]) & own_valid.reshape(
        -1
    )[None, :]
    region_sum = jnp.dot(member.astype(jnp.bfloat16), encoded, preferred_element_type=jnp.float32)
    region_count = jnp.sum(member.astype(jnp.float32), axis=1)
    totals, counted = (
        lax.psum_scatter(region_sum, ("sec", "plane"), scatter_dimension=0, tiled=True),
        lax.psum_scatter(region_count, ("sec", "plane"), scatter_dimension=0, tiled=True),
    )
    pooled = totals / jnp.maximum(counted, 1.0)[:, None]
    return (encoded.reshape(sec_block, tok_block, model_width), pooled)


def solution(mesh):
    in_specs = (
        P(("groups", "sec"), "plane", None),
        P("groups"),
        P(("groups", "sec"), "plane"),
        P(),
        P("plane", None),
        P("plane", None),
        P("plane", None),
        P("plane", None),
    )
    out_specs = (P(("groups", "sec"), "plane", None), P(("groups", "sec", "plane"), None))
    return jax.shard_map(body, mesh=mesh, in_specs=in_specs, out_specs=out_specs, check_vma=False)
```

profile of v0, /device:TPU:8, one launch (start us, length us, event | category | flops | bytes accessed | tf_op | source)
XLA Modules:
  0.0 392.4 jit_solution(481135209715958584)
XLA Ops:
  7.2 1.3 copy-done
  9.4 1.8 constant_dynamic-slice_fusion.1
  11.2 35.6 %all-gather.3.cloned.1.call-done = bf16[1024,768]{1,0:T(8,128)(2,1)} async-done(((bf16[256,768]{1,0:T(8,128)(2,1)}), bf16[1024,768]{1,0:T(8,128)(2,1)}) %all-gather.3.cloned.1.call-update) | async-done | bytes 1572880 | tf_op jit(solution)/shard_map/all_gather | solution.py:45
  46.9 1.5 collective-permute-start
  49.2 18.7 %all_gather.13 = bf16[1024,256]{1,0:T(8,128)(2,1)} all-gather(bf16[256,256]{1,0:T(8,128)(2,1)S(1)} %constant_dynamic-slice_fusion.2), channel_id=1, replica_groups=mesh['groups'=2,'sec'=4,'plane'=4] {'plane'}, dimensions={0}, use_global_device_ids=true | all-gather | bytes 655360 | tf_op jit(solution)/shard_map/all_gather | solution.py:45
  69.2 15.3 %collective-permute-done = bf16[1024,768]{1,0:T(8,128)(2,1)} collective-permute-done((bf16[1024,768]{1,0:T(8,128)(2,1)}, bf16[1024,768]{1,0:T(8,128)(2,1)}, u32[]{:S(2)}, u32[]{:S(2)}) %collective-permute-start) | collective-permute-done | bytes 1572896 | tf_op jit(solution)/shard_map/ppermute | solution.py:50
  84.7 3.6 all-gather.5.cloned.1.call-done
  88.3 1.4 collective-permute-start.8
  89.8 2.0 convolution_dynamic-update-slice_fusion.7
  91.8 2.0 convolution_dynamic-update-slice_fusion.6
  93.8 2.0 convolution_dynamic-update-slice_fusion.5
  95.8 2.0 convolution_dynamic-update-slice_fusion.4
  97.8 1.1 slice_bitcast_fusion.9
  98.9 2.5 collective-permute-start.3
  101.4 1.5 collective-permute-start.4
  103.1 1.7 collective-permute-start.7
  106.4 1.3 copy.57
  107.7 20.3 %collective-permute-done.8 = bf16[1024,768]{1,0:T(8,128)(2,1)} collective-permute-done((bf16[1024,768]{1,0:T(8,128)(2,1)}, bf16[1024,768]{1,0:T(8,128)(2,1)}, u32[]{:S(2)}, u32[]{:S(2)}) %collective-permute-start.8) | collective-permute-done | bytes 1572896 | tf_op jit(solution)/shard_map/ppermute | solution.py:50
  128.5 2.7 pad_maximum_fusion.2
  131.3 2.4 copy.53
  133.7 1.3 copy.51
  135.0 2.0 pad_maximum_fusion
  137.0 1.0 fusion.18
  138.0 3.2 fusion.56
  141.3 1.8 fusion.20
  143.8 1.4 convolution_dynamic-update-slice_fusion.15
  145.2 1.4 convolution_dynamic-update-slice_fusion.14
  146.6 1.4 convolution_dynamic-update-slice_fusion.13
  148.0 1.4 convolution_dynamic-update-slice_fusion.12
  149.8 1.2 copy-done.9
  151.6 2.0 convolution_dynamic-update-slice_fusion.2
  153.7 2.0 convolution_dynamic-update-slice_fusion.1
  155.8 2.0 convolution_dynamic-update-slice_fusion
  159.3 39.7 %all_to_all.45 = bf16[4,8,128,192]{2,3,1,0:T(8,128)(2,1)S(1)} all-to-all(bf16[4,8,128,192]{2,3,1,0:T(8,128)(2,1)S(1)} %bitcast.141), channel_id=1, replica_groups=mesh['groups'=2,'sec'=4,'plane'=4] {'plane'}, dimensions={0} | all-to-all | bytes 3145728 | tf_op jit(solution)/shard_map/all_to_all | solution.py:168
  199.7 5.0 %all-to-all-start = ((bf16[4,8,128]{2,1,0:T(8,128)(2,1)}), bf16[4,8,128]{2,1,0:T(8,128)(2,1)S(1)}, u32[]{:S(2)}, u32[]{:S(2)}) async-start(bf16[4,8,128]{2,1,0:T(8,128)(2,1)} %broadcast_in_dim.86), calls=%async_computation | async-start | bytes 16384 | tf_op jit(solution)/shard_map/all_to_all | solution.py:169
  204.7 2.6 copy.68
  207.3 1.6 all-to-all-done
  208.9 16.5 %while.11 = (s32[]{:T(128)}, bf16[8,512,64]{1,2,0:T(8,128)(2,1)S(1)}, bf16[8,512]{1,0:T(8,128)(2,1)S(1)}, bf16[8,512,192]{2,1,0:T(8,128)(2,1)}, s32[]{:T(128)}) while((s32[]{:T(128)}, bf16[8,512,64]{1,2,0:T(8,128)(2,1)S(1)}, bf16[8,512]{1,0:T(8,128)(2,1)S(1)}, bf16[8,512,192]{2,1,0:T(8,128)(2,1)}, s32[]{:T(128)}) %tuple.52), condition=%wide.region_7.8_spmd.clone, body=%wide.region_4.7_spmd.clone.sunk | while | flops 71336448 | bytes 3945545 | solution.py:98
  211.0 1.0 dynamic-slice_bitcast_fusion.2
  213.0 1.0 dynamic-slice_bitcast_fusion.2
  226.3 1.6 reshape.161
  227.8 4.8 %all-to-all-start.2 = ((bf16[4,2,32768]{2,1,0:T(2,128)(2,1)}), bf16[4,2,32768]{2,1,0:T(2,128)(2,1)S(1)}, u32[]{:S(2)}, u32[]{:S(2)}) async-start(bf16[4,2,32768]{2,1,0:T(2,128)(2,1)} %reshape.161), calls=%async_computation.2 | async-start | bytes 1048576 | tf_op jit(solution)/shard_map/all_to_all | solution.py:172
  233.5 21.6 %all_gather.15 = bf16[1024,256]{1,0:T(8,128)(2,1)S(1)} all-gather(bf16[256,256]{1,0:T(8,128)(2,1)S(1)} %constant_dynamic-slice_fusion), channel_id=1, replica_groups=mesh['groups'=2,'sec'=4,'plane'=4] {'plane'}, dimensions={0}, use_global_device_ids=true | all-gather | bytes 655360 | tf_op jit(solution)/shard_map/all_gather | solution.py:45
  255.2 1.4 collective-permute-start.11
  258.0 30.8 %all-reduce.1 = f32[32]{0:T(128)S(1)} all-reduce(f32[32]{0:T(128)S(1)} %convert_reduce_fusion), channel_id=3, replica_groups=mesh['groups'=2,'sec'=4,'plane'=4] {'sec','plane'}, use_global_device_ids=true, to_apply=%region_10.11.clone | all-reduce | flops 32 | bytes 256
  292.0 1.4 convolution_dynamic-update-slice_fusion.9
  295.0 89.5 %all-reduce.4.cloned.1.call-done = f32[32,1024]{1,0:T(8,128)} async-done(((f32[32,1024]{1,0:T(8,128)}), f32[32,1024]{1,0:T(8,128)}) %all-reduce.4.cloned.1.call-update) | async-done | bytes 131088
  384.5 1.4 dynamic-slice_divide_fusion
  (134 shorter events, 30.9 us)
Async XLA Ops:
  7.2 1.4 copy-start
  7.2 39.7 %all-gather.3.cloned.1.call-start = ((), (), s32[]{:S(2)}) async-start(), calls=%async_computation.3 | async-start | bytes 1966080 | tf_op jit(solution)/shard_map/all_gather | solution.py:45
  8.6 59.7 %copy-start.10 = (s32[8]{0:T(128)S(1)}, s32[8]{0:T(128)}, u32[]{:S(2)}) copy-start(s32[8]{0:T(128)} %param.11) | copy-start | bytes 100
  8.6 60.5 %copy-start.2 = (bf16[2,128,1024]{2,1,0:T(8,128)(2,1)S(1)}, bf16[2,128,1024]{2,1,0:T(8,128)(2,1)}, u32[]{:S(2)}) copy-start(bf16[2,128,1024]{2,1,0:T(8,128)(2,1)} %param.10) | copy-start | bytes 1572868
  9.4 75.1 %copy-start.7 = (f32[2,1024]{1,0:T(2,128)S(1)}, f32[2,1024]{1,0:T(2,128)}, u32[]{:S(2)}) copy-start(f32[2,1024]{1,0:T(2,128)} %param.13) | copy-start | bytes 24580
  9.4 78.9 %all-gather.5.cloned.1.call-start = ((), (), s32[]{:S(2)}) async-start(), calls=%async_computation.4 | async-start | bytes 1966080 | tf_op jit(solution)/shard_map/all_gather | solution.py:45
  46.9 37.6 %collective-permute-start = (bf16[1024,768]{1,0:T(8,128)(2,1)}, bf16[1024,768]{1,0:T(8,128)(2,1)}, u32[]{:S(2)}, u32[]{:S(2)}) collective-permute-start(bf16[1024,768]{1,0:T(8,128)(2,1)} %all-gather.3.cloned.1.call-done), channel_id=1, source_target_pairs={{0,16},{16,0},{1,17},{17,1},{2,18},{18,2},{3,19},{19,3},{4,20},{20... | collective-permute-start | bytes 4718600 | tf_op jit(solution)/shard_map/ppermute | solution.py:50
  67.9 35.1 %collective-permute-start.5 = (bf16[1024,256]{1,0:T(8,128)(2,1)}, bf16[1024,256]{1,0:T(8,128)(2,1)}, u32[]{:S(2)}, u32[]{:S(2)}) collective-permute-start(bf16[1024,256]{1,0:T(8,128)(2,1)} %all_gather.13), channel_id=1, source_target_pairs={{0,16},{16,0},{1,17},{17,1},{2,18},{18,2},{3,19},{19,3},{4,20},{20... | collective-permute-start | bytes 1572872 | tf_op jit(solution)/shard_map/ppermute | solution.py:50
  68.3 78.3 %collective-permute-start.6 = (bf16[1024,256]{1,0:T(8,128)(2,1)}, bf16[1024,256]{1,0:T(8,128)(2,1)}, u32[]{:S(2)}, u32[]{:S(2)}) collective-permute-start(bf16[1024,256]{1,0:T(8,128)(2,1)} %all_gather.13), channel_id=1, source_target_pairs={{0,4},{4,0},{8,12},{12,8},{1,5},{5,1},{9,13},{13,9},{2,6},{6,2},{1... | collective-permute-start | bytes 1572872 | tf_op jit(solution)/shard_map/ppermute | solution.py:55
  68.5 25.3 %collective-permute-start.1 = (bf16[1024,768]{1,0:T(8,128)(2,1)}, bf16[1024,768]{1,0:T(8,128)(2,1)}, u32[]{:S(2)}, u32[]{:S(2)}) collective-permute-start(bf16[1024,768]{1,0:T(8,128)(2,1)} %all-gather.3.cloned.1.call-done), channel_id=1, source_target_pairs={{0,4},{4,0},{8,12},{12,8},{1,5},{5,1},{9,13},{13,9},{2,6},{6,2},{1... | collective-permute-start | bytes 4718600 | tf_op jit(solution)/shard_map/ppermute | solution.py:55
  84.5 11.3 %collective-permute-start.2 = (bf16[1024,768]{1,0:T(8,128)(2,1)}, bf16[1024,768]{1,0:T(8,128)(2,1)}, u32[]{:S(2)}, u32[]{:S(2)}) collective-permute-start(bf16[1024,768]{1,0:T(8,128)(2,1)} %collective-permute-done), channel_id=1, source_target_pairs={{0,4},{4,0},{8,12},{12,8},{1,5},{5,1},{9,13},{13,9},{2,6},{6,2},{1... | collective-permute-start | bytes 4718600 | tf_op jit(solution)/shard_map/ppermute | solution.py:55
  88.3 39.8 %collective-permute-start.8 = (bf16[1024,768]{1,0:T(8,128)(2,1)}, bf16[1024,768]{1,0:T(8,128)(2,1)}, u32[]{:S(2)}, u32[]{:S(2)}) collective-permute-start(bf16[1024,768]{1,0:T(8,128)(2,1)} %all-gather.5.cloned.1.call-done), channel_id=1, source_target_pairs={{0,16},{16,0},{1,17},{17,1},{2,18},{18,2},{3,19},{19,3},{4,20},{20... | collective-permute-start | bytes 4718600 | tf_op jit(solution)/shard_map/ppermute | solution.py:50
  98.9 29.1 %collective-permute-start.3 = (bf16[128,2048]{1,0:T(8,128)(2,1)}, bf16[128,2048]{1,0:T(8,128)(2,1)}, u32[]{:S(2)}, u32[]{:S(2)}) collective-permute-start(bf16[128,2048]{1,0:T(8,128)(2,1)} %get-tuple-element.85), channel_id=1, source_target_pairs={{0,4},{4,8},{8,12},{1,5},{5,9},{9,13},{2,6},{6,10},{10,14},{3,7},{... | collective-permute-start | bytes 1572872 | tf_op jit(solution)/shard_map/ppermute | solution.py:16
  101.4 27.1 %collective-permute-start.4 = (bf16[128,2048]{1,0:T(8,128)(2,1)}, bf16[128,2048]{1,0:T(8,128)(2,1)}, u32[]{:S(2)}, u32[]{:S(2)}) collective-permute-start(bf16[128,2048]{1,0:T(8,128)(2,1)} %get-tuple-element.86), channel_id=1, source_target_pairs={{4,0},{8,4},{12,8},{5,1},{9,5},{13,9},{6,2},{10,6},{14,10},{7,3},{... | collective-permute-start | bytes 1572872 | tf_op jit(solution)/shard_map/ppermute | solution.py:16
  103.1 44.9 %collective-permute-start.7 = (bf16[1024,256]{1,0:T(8,128)(2,1)}, bf16[1024,256]{1,0:T(8,128)(2,1)}, u32[]{:S(2)}, u32[]{:S(2)}) collective-permute-start(bf16[1024,256]{1,0:T(8,128)(2,1)} %collective-permute-done.5), channel_id=1, source_target_pairs={{0,4},{4,0},{8,12},{12,8},{1,5},{5,1},{9,13},{13,9},{2,6},{6,2},{1... | collective-permute-start | bytes 1572872 | tf_op jit(solution)/shard_map/ppermute | solution.py:55
  128.0 25.7 %collective-permute-start.9 = (bf16[1024,768]{1,0:T(8,128)(2,1)}, bf16[1024,768]{1,0:T(8,128)(2,1)}, u32[]{:S(2)}, u32[]{:S(2)}) collective-permute-start(bf16[1024,768]{1,0:T(8,128)(2,1)} %all-gather.5.cloned.1.call-done), channel_id=1, source_target_pairs={{0,4},{4,0},{8,12},{12,8},{1,5},{5,1},{9,13},{13,9},{2,6},{6,2},{1... | collective-permute-start | bytes 4718600 | tf_op jit(solution)/shard_map/ppermute | solution.py:55
  128.0 27.7 %collective-permute-start.10 = (bf16[1024,768]{1,0:T(8,128)(2,1)}, bf16[1024,768]{1,0:T(8,128)(2,1)}, u32[]{:S(2)}, u32[]{:S(2)}) collective-permute-start(bf16[1024,768]{1,0:T(8,128)(2,1)} %collective-permute-done.8), channel_id=1, source_target_pairs={{0,4},{4,0},{8,12},{12,8},{1,5},{5,1},{9,13},{13,9},{2,6},{6,2},{1... | collective-permute-start | bytes 4718600 | tf_op jit(solution)/shard_map/ppermute | solution.py:55
  131.3 2.4 copy-start.3
  149.4 1.6 copy-start.9
  149.6 6.1 %copy-start.5 = (bf16[256,1024]{1,0:T(8,128)(2,1)}, bf16[256,1024]{1,0:T(8,128)(2,1)S(1)}, u32[]{:S(2)}) copy-start(bf16[256,1024]{1,0:T(8,128)(2,1)S(1)} %get-tuple-element.82) | copy-start | bytes 1572868
  199.7 9.2 %all-to-all-start = ((bf16[4,8,128]{2,1,0:T(8,128)(2,1)}), bf16[4,8,128]{2,1,0:T(8,128)(2,1)S(1)}, u32[]{:S(2)}, u32[]{:S(2)}) async-start(bf16[4,8,128]{2,1,0:T(8,128)(2,1)} %broadcast_in_dim.86), calls=%async_computation | async-start | bytes 16384 | tf_op jit(solution)/shard_map/all_to_all | solution.py:169
  226.2 30.4 %copy-start.8 = (s32[2,128]{1,0:T(2,128)S(1)}, s32[2,128]{1,0:T(2,128)}, u32[]{:S(2)}) copy-start(s32[2,128]{1,0:T(2,128)} %param.12) | copy-start | bytes 3076
  226.2 30.5 %copy-start.11 = (u32[32]{0:T(128)S(1)}, u32[32]{0:T(128)}, u32[]{:S(2)}) copy-start(u32[32]{0:T(128)} %constant.117) | copy-start | bytes 388
  227.8 61.1 %all-to-all-start.2 = ((bf16[4,2,32768]{2,1,0:T(2,128)(2,1)}), bf16[4,2,32768]{2,1,0:T(2,128)(2,1)S(1)}, u32[]{:S(2)}, u32[]{:S(2)}) async-start(bf16[4,2,32768]{2,1,0:T(2,128)(2,1)} %reshape.161), calls=%async_computation.2 | async-start | bytes 1048576 | tf_op jit(solution)/shard_map/all_to_all | solution.py:172
  232.6 151.8 %all-reduce.4.cloned.1.call-start = ((), (), s32[]{:S(2)}) async-start(), calls=%async_computation.5 | async-start | bytes 262144
  255.2 33.7 %collective-permute-start.11 = (bf16[1024,256]{1,0:T(8,128)(2,1)S(1)}, bf16[1024,256]{1,0:T(8,128)(2,1)S(1)}, u32[]{:S(2)}, u32[]{:S(2)}) collective-permute-start(bf16[1024,256]{1,0:T(8,128)(2,1)S(1)} %all_gather.15), channel_id=1, source_target_pairs={{0,16},{16,0},{1,17},{17,1},{2,18},{18,2},{3,19},{19,3},{4,20},{20... | collective-permute-start | bytes 1572872 | tf_op jit(solution)/shard_map/ppermute | solution.py:50
  256.6 35.4 %collective-permute-start.12 = (bf16[1024,256]{1,0:T(8,128)(2,1)S(1)}, bf16[1024,256]{1,0:T(8,128)(2,1)}, u32[]{:S(2)}, u32[]{:S(2)}) collective-permute-start(bf16[1024,256]{1,0:T(8,128)(2,1)S(1)} %all_gather.15), channel_id=1, source_target_pairs={{0,4},{4,0},{8,12},{12,8},{1,5},{5,1},{9,13},{13,9},{2,6},{6,2},{1... | collective-permute-start | bytes 1572872 | tf_op jit(solution)/shard_map/ppermute | solution.py:55
  288.9 4.7 %collective-permute-start.13 = (bf16[1024,256]{1,0:T(8,128)(2,1)S(1)}, bf16[1024,256]{1,0:T(8,128)(2,1)S(1)}, u32[]{:S(2)}, u32[]{:S(2)}) collective-permute-start(bf16[1024,256]{1,0:T(8,128)(2,1)S(1)} %collective-permute-done.11), channel_id=1, source_target_pairs={{0,4},{4,0},{8,12},{12,8},{1,5},{5,1},{9,13},{13,9},{2,6},{6,2},{1... | collective-permute-start | bytes 1572872 | tf_op jit(solution)/shard_map/ppermute | solution.py:55
  292.0 1.9 copy-start.6
  293.5 92.4 %copy-start.1 = (bf16[256,3072]{1,0:T(8,128)(2,1)S(1)}, bf16[256,3072]{1,0:T(8,128)(2,1)}, u32[]{:S(2)}) copy-start(bf16[256,3072]{1,0:T(8,128)(2,1)} %param.14) | copy-start | bytes 4718596
  294.0 91.9 %copy-start.4 = (bf16[256,1024]{1,0:T(8,128)(2,1)}, bf16[256,1024]{1,0:T(8,128)(2,1)S(1)}, u32[]{:S(2)}) copy-start(bf16[256,1024]{1,0:T(8,128)(2,1)S(1)} %fusion.24) | copy-start | bytes 1572868
Sparse Core Ops, SparseCore 0:
  9.6 37.2 all-gather.2
  49.0 39.2 all-gather.4
  295.0 89.3 all-reduce.3
where the time goes:
time: 394 us; the launch traced here: 392 us
  waiting for transfers between devices  166 us (42%)
  blocking collectives  111 us (28%)
  local copies, waits for them, and re-layouts  33.4 us (8%)
  matrix products  32.7 us (8%)
  starting transfers between devices  21.3 us (5%)
  between operations  15 us (4%)
  other arithmetic  12.9 us (3%)
    unnamed x4, waiting for transfers between devices  89.5 us
    all_gather x2, blocking collectives, gather_pieces(): first = lax.all_gather(mine, 'plane', axis=0, tiled=True)  40.4 us
    all_to_all x1, blocking collectives, body(): lax.all_to_all(heads_first, 'plane', split_axis=0, concat_axis=2, tiled=T...  39.7 us
    all_gather x2, waiting for transfers between devices, gather_pieces(): first = lax.all_gather(mine, 'plane', axis=0, tiled=True)  39.2 us
    ppermute x4, waiting for transfers between devices, gather_pieces(): by_group.append((source * pair + k, lax.ppermute(first, 'groups', moved)))  35.6 us
    unnamed x1, blocking collectives  30.8 us
    dot_general x16, matrix products, project(): part = jnp.dot(inputs, block, preferred_element_type=jnp.float32)  22.8 us
    unnamed x29, local copies, waits for them, and re-layouts  8.08 us
  transfers between devices with their start and end apart: 19, of which 6 were waited for; matrix products, arithmetic and copies ran while one was open for 13% of the time, Pallas kernels for 0%

commit v1 on v0

--- a/solution.py
+++ b/solution.py
@@ -8,6 +8,27 @@
 HEAD_DIM = 64
 WINDOW = 128
 negative_big = -1e30
+
+
+def ring_gather(x, axis, dim):
+    devices, index, rows = (lax.axis_size(axis), lax.axis_index(axis), x.shape[dim])
+    right = [(i, (i + 1) % devices) for i in range(devices)]
+    left = [(i, (i - 1) % devices) for i in range(devices)]
+    out = jnp.zeros((*x.shape[:dim], devices * rows, *x.shape[dim + 1 :]), x.dtype)
+    out = lax.dynamic_update_slice_in_dim(out, x, index * rows, axis=dim)
+    from_left = from_right = x
+    middle = devices // 2
+    for step in range(1, middle + 1):
+        from_left = lax.ppermute(from_left, axis, right)
+        out = lax.dynamic_update_slice_in_dim(
+            out, from_left, (index - step) % devices * rows, axis=dim
+        )
+        if step < devices - middle:
+            from_right = lax.ppermute(from_right, axis, left)
+            out = lax.dynamic_update_slice_in_dim(
+                out, from_right, (index + step) % devices * rows, axis=dim
+            )
+    return out
 
 
 def shifted_2(value, axis, by):
@@ -42,7 +63,7 @@
     k = lax.axis_index("sec") % pair
     own = g * pair + k
     mine = lax.dynamic_slice_in_dim(shard, own * width, width, axis=1)
-    first = lax.all_gather(mine, "plane", axis=0, tiled=True)
+    first = ring_gather(mine, "plane", 0)
     by_group = [(own, first)]
     for step in range(1, groups):
         moved = [(i, (i + step) % groups) for i in range(groups)]

time: 394 us -> 379 us (0.962)
  blocking collectives: 111 us -> 30.8 us
  starting transfers between devices: 21.3 us -> 53.5 us
  waiting for transfers between devices: 166 us -> 188 us
  local copies, waits for them, and re-layouts: 33.4 us -> 44.4 us
    all_gather x2 -> x0, blocking collectives: 40.4 us -> none  [gather_pieces(): first = lax.all_gather(mine, 'plane', axis=0, tiled=True)]
    all_to_all x1 -> x0, blocking collectives: 39.7 us -> none  [body(): lax.all_to_all(heads_first, 'plane', split_axis=0, concat_axis=2, tiled=T...]
    all_gather x2 -> x0, waiting for transfers between devices: 39.2 us -> none  [gather_pieces(): first = lax.all_gather(mine, 'plane', axis=0, tiled=True)]
    all_to_all x0 -> x1, waiting for transfers between devices: none -> 32.6 us  [body(): lax.all_to_all(heads_first, 'plane', split_axis=0, concat_axis=2, tiled=T...]
    ppermute x0 -> x12, starting transfers between devices: none -> 19.8 us  [the longest x8 16.8 us: ring_gather(): from_left = lax.ppermute(from_left, axis, right)]
    ppermute x0 -> x12, waiting for transfers between devices: none -> 16.5 us  [the longest x8 16.5 us: ring_gather(): from_left = lax.ppermute(from_left, axis, right)]
    dynamic_update_slice x0 -> x16, local copies, waits for them, and re-layouts: none -> 14.4 us  [the longest x4 6.17 us: ring_gather(): out = lax.dynamic_update_slice_in_dim(out, x, index * rows, axis=dim)]
    ppermute x4, waiting for transfers between devices: 35.6 us -> 48.3 us  [gather_pieces(): by_group.append((source * pair + k, lax.ppermute(first, 'groups', moved)))]
  transfers between devices with their start and end apart: 19 -> 30, of which waited for: 6 -> 7; matrix products, arithmetic and copies ran while one was open for 13% -> 21% of each run, Pallas kernels for 0% -> 0%
where the time goes in v1:
time: 379 us; the launch traced here: 377 us
  waiting for transfers between devices  188 us (50%)
  starting transfers between devices  53.5 us (14%)
  local copies, waits for them, and re-layouts  44.4 us (12%)
  matrix products  31.2 us (8%)
  blocking collectives  30.8 us (8%)
  between operations  15.3 us (4%)
  other arithmetic  14.2 us (4%)
    unnamed x2, waiting for transfers between devices  90.1 us
    ppermute x4, waiting for transfers between devices, gather_pieces(): by_group.append((source * pair + k, lax.ppermute(first, 'groups', moved)))  48.3 us
    all_to_all x1, waiting for transfers between devices, body(): lax.all_to_all(heads_first, 'plane', split_axis=0, concat_axis=2, tiled=T...  32.6 us
    unnamed x1, blocking collectives  30.8 us
    dot_general x16, matrix products, project(): part = jnp.dot(inputs, block, preferred_element_type=jnp.float32)  21.3 us
    ppermute x8, starting transfers between devices, ring_gather(): from_left = lax.ppermute(from_left, axis, right)  16.8 us
    ppermute x8, waiting for transfers between devices, ring_gather(): from_left = lax.ppermute(from_left, axis, right)  16.5 us
    all_to_all x1, starting transfers between devices, body(): lax.all_to_all(key_flags, 'plane', split_axis=0, concat_axis=2, tiled=True)  8.02 us
  transfers between devices with their start and end apart: 30, of which 7 were waited for; matrix products, arithmetic and copies ran while one was open for 21% of the time, Pallas kernels for 0%

profile of v1, /device:TPU:8, one launch (start us, length us, event | category | flops | bytes accessed | tf_op | source)
XLA Modules:
  0.0 377.2 jit_solution(3114133574908750699)
XLA Ops:
  7.3 1.8 constant_dynamic-update-slice_fusion.15
  9.1 1.6 collective-permute-start
  11.1 10.2 %collective-permute-done = bf16[256,768]{1,0:T(8,128)(2,1)S(1)} collective-permute-done((bf16[256,768]{1,0:T(8,128)(2,1)}, bf16[256,768]{1,0:T(8,128)(2,1)S(1)}, u32[]{:S(2)}, u32[]{:S(2)}) %collective-permute-start) | collective-permute-done | bytes 393248 | tf_op jit(solution)/shard_map/ppermute | solution.py:22
  21.3 7.8 %collective-permute-start.2 = (bf16[256,768]{1,0:T(8,128)(2,1)S(1)}, bf16[256,768]{1,0:T(8,128)(2,1)}, u32[]{:S(2)}, u32[]{:S(2)}) collective-permute-start(bf16[256,768]{1,0:T(8,128)(2,1)S(1)} %collective-permute-done), channel_id=1, source_target_pairs={{0,1},{1,2},{2,3},{3,0},{4,5},{5,6},{6,7},{7,4},{8,9},{9,10},{10,1... | collective-permute-start | bytes 1179656 | tf_op jit(solution)/shard_map/ppermute | solution.py:22
  29.9 1.6 constant_dynamic-update-slice_fusion.11
  31.5 1.7 collective-permute-start.8
  34.8 1.9 constant_dynamic-update-slice_fusion.7
  36.7 1.7 collective-permute-start.14
  40.5 1.6 collective-permute-start.3
  44.3 2.2 collective-permute-start.15
  46.9 26.7 %collective-permute-done.3 = bf16[1024,768]{1,0:T(8,128)(2,1)} collective-permute-done((bf16[1024,768]{1,0:T(8,128)(2,1)S(1)}, bf16[1024,768]{1,0:T(8,128)(2,1)}, u32[]{:S(2)}, u32[]{:S(2)}) %collective-permute-start.3) | collective-permute-done | bytes 1572896 | tf_op jit(solution)/shard_map/ppermute | solution.py:71
  73.6 1.6 constant_dynamic-update-slice_fusion.10
  75.4 1.6 constant_dynamic-update-slice_fusion.9
  77.6 1.5 collective-permute-start.11
  80.7 6.1 %collective-permute-done.16 = bf16[256,768]{1,0:T(8,128)(2,1)S(1)} collective-permute-done((bf16[256,768]{1,0:T(8,128)(2,1)S(1)}, bf16[256,768]{1,0:T(8,128)(2,1)S(1)}, u32[]{:S(2)}, u32[]{:S(2)}) %collective-permute-start.16) | collective-permute-done | bytes 393248 | tf_op jit(solution)/shard_map/ppermute | solution.py:22
  87.5 1.5 collective-permute-start.17
  89.8 2.0 convolution_dynamic-update-slice_fusion.6
  91.8 2.0 convolution_dynamic-update-slice_fusion.5
  95.5 2.3 collective-permute-start.6
  97.8 1.5 collective-permute-start.7
  99.4 1.9 collective-permute-start.12
  104.3 21.5 %collective-permute-done.17 = bf16[1024,768]{1,0:T(8,128)(2,1)} collective-permute-done((bf16[1024,768]{1,0:T(8,128)(2,1)}, bf16[1024,768]{1,0:T(8,128)(2,1)}, u32[]{:S(2)}, u32[]{:S(2)}) %collective-permute-start.17) | collective-permute-done | bytes 1572896 | tf_op jit(solution)/shard_map/ppermute | solution.py:71
  126.3 2.8 pad_maximum_fusion.2
  129.1 2.4 copy.53
  132.8 2.0 pad_maximum_fusion
  135.9 3.2 fusion.56
  139.1 1.8 fusion.20
  141.6 1.4 convolution_dynamic-update-slice_fusion.15
  143.0 1.4 convolution_dynamic-update-slice_fusion.14
  145.8 1.4 convolution_dynamic-update-slice_fusion.12
  147.7 2.0 convolution_dynamic-update-slice_fusion.3
  149.7 2.0 convolution_dynamic-update-slice_fusion.2
  151.8 2.0 convolution_dynamic-update-slice_fusion.1
  153.8 2.0 convolution_dynamic-update-slice_fusion
  157.0 1.6 copy.60
  158.6 6.1 %all-to-all-start.1 = ((bf16[4,8,128,192]{2,3,1,0:T(8,128)(2,1)}), bf16[4,8,128,192]{2,3,1,0:T(8,128)(2,1)S(1)}, u32[]{:S(2)}, u32[]{:S(2)}) async-start(bf16[4,8,128,192]{2,3,1,0:T(8,128)(2,1)} %bitcast.26), calls=%async_computation.1 | async-start | bytes 3145728 | tf_op jit(solution)/shard_map/all_to_all | solution.py:189
  165.7 1.5 collective-permute-start.20
  167.2 32.6 %all-to-all-done.1 = bf16[4,8,128,192]{2,3,1,0:T(8,128)(2,1)S(1)} async-done(((bf16[4,8,128,192]{2,3,1,0:T(8,128)(2,1)}), bf16[4,8,128,192]{2,3,1,0:T(8,128)(2,1)S(1)}, u32[]{:S(2)}, u32[]{:S(2)}) %all-to-all-start.1) | async-done | bytes 1572896 | tf_op jit(solution)/shard_map/all_to_all | solution.py:189
  200.5 8.0 %all-to-all-start = ((bf16[4,8,128]{2,1,0:T(8,128)(2,1)}), bf16[4,8,128]{2,1,0:T(8,128)(2,1)S(1)}, u32[]{:S(2)}, u32[]{:S(2)}) async-start(bf16[4,8,128]{2,1,0:T(8,128)(2,1)} %broadcast_in_dim.86), calls=%async_computation | async-start | bytes 16384 | tf_op jit(solution)/shard_map/all_to_all | solution.py:190
  208.6 1.9 collective-permute-start.22
  210.5 2.6 copy.68
  213.1 16.5 %while.11 = (s32[]{:T(128)}, bf16[8,512,64]{1,2,0:T(8,128)(2,1)S(1)}, bf16[8,512]{1,0:T(8,128)(2,1)S(1)}, bf16[8,512,192]{2,1,0:T(8,128)(2,1)}, s32[]{:T(128)}) while((s32[]{:T(128)}, bf16[8,512,64]{1,2,0:T(8,128)(2,1)S(1)}, bf16[8,512]{1,0:T(8,128)(2,1)S(1)}, bf16[8,512,192]{2,1,0:T(8,128)(2,1)}, s32[]{:T(128)}) %tuple.52), condition=%wide.region_7.8_spmd.clone, body=%wide.region_4.7_spmd.clone.sunk | while | flops 71336448 | bytes 3945545 | solution.py:119
  230.5 1.6 reshape.161
  232.0 6.9 %all-to-all-start.2 = ((bf16[4,2,32768]{2,1,0:T(2,128)(2,1)}), bf16[4,2,32768]{2,1,0:T(2,128)(2,1)S(1)}, u32[]{:S(2)}, u32[]{:S(2)}) async-start(bf16[4,2,32768]{2,1,0:T(2,128)(2,1)} %reshape.161), calls=%async_computation.2 | async-start | bytes 1048576 | tf_op jit(solution)/shard_map/all_to_all | solution.py:193
  239.0 1.6 collective-permute-start.23
  242.0 30.8 %all-reduce.1 = f32[32]{0:T(128)S(1)} all-reduce(f32[32]{0:T(128)S(1)} %convert_reduce_fusion), channel_id=3, replica_groups=mesh['groups'=2,'sec'=4,'plane'=4] {'sec','plane'}, use_global_device_ids=true, to_apply=%region_10.11.clone | all-reduce | flops 32 | bytes 256
  278.8 90.1 %all-reduce.4.cloned.1.call-done = f32[32,1024]{1,0:T(8,128)} async-done(((f32[32,1024]{1,0:T(8,128)}), f32[32,1024]{1,0:T(8,128)}) %all-reduce.4.cloned.1.call-update) | async-done | bytes 131088
  368.9 1.4 dynamic-slice_divide_fusion
  (163 shorter events, 48.2 us)
Async XLA Ops:
  9.1 12.2 %collective-permute-start = (bf16[256,768]{1,0:T(8,128)(2,1)}, bf16[256,768]{1,0:T(8,128)(2,1)S(1)}, u32[]{:S(2)}, u32[]{:S(2)}) collective-permute-start(bf16[256,768]{1,0:T(8,128)(2,1)} %get-tuple-element.84), channel_id=1, source_target_pairs={{0,1},{1,2},{2,3},{3,0},{4,5},{5,6},{6,7},{7,4},{8,9},{9,10},{10,1... | collective-permute-start | bytes 1179656 | tf_op jit(solution)/shard_map/ppermute | solution.py:22
  10.7 27.7 %collective-permute-start.1 = (bf16[256,768]{1,0:T(8,128)(2,1)}, bf16[256,768]{1,0:T(8,128)(2,1)}, u32[]{:S(2)}, u32[]{:S(2)}) collective-permute-start(bf16[256,768]{1,0:T(8,128)(2,1)} %get-tuple-element.84), channel_id=1, source_target_pairs={{0,3},{1,0},{2,1},{3,2},{4,7},{5,4},{6,5},{7,6},{8,11},{9,8},{10,9... | collective-permute-start | bytes 1179656 | tf_op jit(solution)/shard_map/ppermute | solution.py:27
  21.3 18.1 %collective-permute-start.2 = (bf16[256,768]{1,0:T(8,128)(2,1)S(1)}, bf16[256,768]{1,0:T(8,128)(2,1)}, u32[]{:S(2)}, u32[]{:S(2)}) collective-permute-start(bf16[256,768]{1,0:T(8,128)(2,1)S(1)} %collective-permute-done), channel_id=1, source_target_pairs={{0,1},{1,2},{2,3},{3,0},{4,5},{5,6},{6,7},{7,4},{8,9},{9,10},{10,1... | collective-permute-start | bytes 1179656 | tf_op jit(solution)/shard_map/ppermute | solution.py:22
  31.5 12.8 %collective-permute-start.8 = (bf16[256,256]{1,0:T(8,128)(2,1)S(1)}, bf16[256,256]{1,0:T(8,128)(2,1)}, u32[]{:S(2)}, u32[]{:S(2)}) collective-permute-start(bf16[256,256]{1,0:T(8,128)(2,1)S(1)} %get-tuple-element.86), channel_id=1, source_target_pairs={{0,1},{1,2},{2,3},{3,0},{4,5},{5,6},{6,7},{7,4},{8,9},{9,10},{10,1... | collective-permute-start | bytes 393224 | tf_op jit(solution)/shard_map/ppermute | solution.py:22
  33.2 13.3 %collective-permute-start.9 = (bf16[256,256]{1,0:T(8,128)(2,1)S(1)}, bf16[256,256]{1,0:T(8,128)(2,1)}, u32[]{:S(2)}, u32[]{:S(2)}) collective-permute-start(bf16[256,256]{1,0:T(8,128)(2,1)S(1)} %get-tuple-element.86), channel_id=1, source_target_pairs={{0,3},{1,0},{2,1},{3,2},{4,7},{5,4},{6,5},{7,6},{8,11},{9,8},{10,9... | collective-permute-start | bytes 393224 | tf_op jit(solution)/shard_map/ppermute | solution.py:27
  34.8 7.3 %copy-start.8 = (s32[8]{0:T(128)S(1)}, s32[8]{0:T(128)}, u32[]{:S(2)}) copy-start(s32[8]{0:T(128)} %param.11) | copy-start | bytes 100
  34.8 7.4 %copy-start = (bf16[2,128,1024]{2,1,0:T(8,128)(2,1)S(1)}, bf16[2,128,1024]{2,1,0:T(8,128)(2,1)}, u32[]{:S(2)}) copy-start(bf16[2,128,1024]{2,1,0:T(8,128)(2,1)} %param.10) | copy-start | bytes 1572868
  36.7 5.8 %copy-start.5 = (f32[2,1024]{1,0:T(2,128)S(1)}, f32[2,1024]{1,0:T(2,128)}, u32[]{:S(2)}) copy-start(f32[2,1024]{1,0:T(2,128)} %param.13) | copy-start | bytes 24580
  36.7 38.5 %collective-permute-start.14 = (bf16[256,768]{1,0:T(8,128)(2,1)S(1)}, bf16[256,768]{1,0:T(8,128)(2,1)S(1)}, u32[]{:S(2)}, u32[]{:S(2)}) collective-permute-start(bf16[256,768]{1,0:T(8,128)(2,1)S(1)} %get-tuple-element.88), channel_id=1, source_target_pairs={{0,1},{1,2},{2,3},{3,0},{4,5},{5,6},{6,7},{7,4},{8,9},{9,10},{10,1... | collective-permute-start | bytes 1179656 | tf_op jit(solution)/shard_map/ppermute | solution.py:22
  40.5 33.1 %collective-permute-start.3 = (bf16[1024,768]{1,0:T(8,128)(2,1)S(1)}, bf16[1024,768]{1,0:T(8,128)(2,1)}, u32[]{:S(2)}, u32[]{:S(2)}) collective-permute-start(bf16[1024,768]{1,0:T(8,128)(2,1)S(1)} %constant_dynamic-update-slice_fusion.12), channel_id=1, source_target_pairs={{0,16},{16,0},{1,17},{17,1},{2,18},{18,2},{3,19},{19,3},{4,20},{20... | collective-permute-start | bytes 4718600 | tf_op jit(solution)/shard_map/ppermute | solution.py:71
  42.7 49.1 %collective-permute-start.4 = (bf16[1024,768]{1,0:T(8,128)(2,1)S(1)}, bf16[1024,768]{1,0:T(8,128)(2,1)}, u32[]{:S(2)}, u32[]{:S(2)}) collective-permute-start(bf16[1024,768]{1,0:T(8,128)(2,1)S(1)} %constant_dynamic-update-slice_fusion.12), channel_id=1, source_target_pairs={{0,4},{4,0},{8,12},{12,8},{1,5},{5,1},{9,13},{13,9},{2,6},{6,2},{1... | collective-permute-start | bytes 4718600 | tf_op jit(solution)/shard_map/ppermute | solution.py:76
  44.3 35.6 %collective-permute-start.15 = (bf16[256,768]{1,0:T(8,128)(2,1)S(1)}, bf16[256,768]{1,0:T(8,128)(2,1)S(1)}, u32[]{:S(2)}, u32[]{:S(2)}) collective-permute-start(bf16[256,768]{1,0:T(8,128)(2,1)S(1)} %get-tuple-element.88), channel_id=1, source_target_pairs={{0,3},{1,0},{2,1},{3,2},{4,7},{5,4},{6,5},{7,6},{8,11},{9,8},{10,9... | collective-permute-start | bytes 1179656 | tf_op jit(solution)/shard_map/ppermute | solution.py:27
  46.5 30.5 %collective-permute-start.10 = (bf16[256,256]{1,0:T(8,128)(2,1)}, bf16[256,256]{1,0:T(8,128)(2,1)S(1)}, u32[]{:S(2)}, u32[]{:S(2)}) collective-permute-start(bf16[256,256]{1,0:T(8,128)(2,1)} %collective-permute-done.8), channel_id=1, source_target_pairs={{0,1},{1,2},{2,3},{3,0},{4,5},{5,6},{6,7},{7,4},{8,9},{9,10},{10,1... | collective-permute-start | bytes 393224 | tf_op jit(solution)/shard_map/ppermute | solution.py:22
  73.6 20.1 %collective-permute-start.5 = (bf16[1024,768]{1,0:T(8,128)(2,1)}, bf16[1024,768]{1,0:T(8,128)(2,1)S(1)}, u32[]{:S(2)}, u32[]{:S(2)}) collective-permute-start(bf16[1024,768]{1,0:T(8,128)(2,1)} %collective-permute-done.3), channel_id=1, source_target_pairs={{0,4},{4,0},{8,12},{12,8},{1,5},{5,1},{9,13},{13,9},{2,6},{6,2},{1... | collective-permute-start | bytes 4718600 | tf_op jit(solution)/shard_map/ppermute | solution.py:76
  75.2 11.5 %collective-permute-start.16 = (bf16[256,768]{1,0:T(8,128)(2,1)S(1)}, bf16[256,768]{1,0:T(8,128)(2,1)S(1)}, u32[]{:S(2)}, u32[]{:S(2)}) collective-permute-start(bf16[256,768]{1,0:T(8,128)(2,1)S(1)} %collective-permute-done.14), channel_id=1, source_target_pairs={{0,1},{1,2},{2,3},{3,0},{4,5},{5,6},{6,7},{7,4},{8,9},{9,10},{10,1... | collective-permute-start | bytes 1179656 | tf_op jit(solution)/shard_map/ppermute | solution.py:22
  77.6 23.7 %collective-permute-start.11 = (bf16[1024,256]{1,0:T(8,128)(2,1)}, bf16[1024,256]{1,0:T(8,128)(2,1)}, u32[]{:S(2)}, u32[]{:S(2)}) collective-permute-start(bf16[1024,256]{1,0:T(8,128)(2,1)} %constant_dynamic-update-slice_fusion.8), channel_id=1, source_target_pairs={{0,16},{16,0},{1,17},{17,1},{2,18},{18,2},{3,19},{19,3},{4,20},{20... | collective-permute-start | bytes 1572872 | tf_op jit(solution)/shard_map/ppermute | solution.py:71
  87.5 38.3 %collective-permute-start.17 = (bf16[1024,768]{1,0:T(8,128)(2,1)}, bf16[1024,768]{1,0:T(8,128)(2,1)}, u32[]{:S(2)}, u32[]{:S(2)}) collective-permute-start(bf16[1024,768]{1,0:T(8,128)(2,1)} %constant_dynamic-update-slice_fusion.4), channel_id=1, source_target_pairs={{0,16},{16,0},{1,17},{17,1},{2,18},{18,2},{3,19},{19,3},{4,20},{20... | collective-permute-start | bytes 4718600 | tf_op jit(solution)/shard_map/ppermute | solution.py:71
  95.5 30.4 %collective-permute-start.6 = (bf16[128,2048]{1,0:T(8,128)(2,1)}, bf16[128,2048]{1,0:T(8,128)(2,1)}, u32[]{:S(2)}, u32[]{:S(2)}) collective-permute-start(bf16[128,2048]{1,0:T(8,128)(2,1)} %get-tuple-element.93), channel_id=1, source_target_pairs={{0,4},{4,8},{8,12},{1,5},{5,9},{9,13},{2,6},{6,10},{10,14},{3,7},{... | collective-permute-start | bytes 1572872 | tf_op jit(solution)/shard_map/ppermute | solution.py:37
  97.8 28.5 %collective-permute-start.7 = (bf16[128,2048]{1,0:T(8,128)(2,1)}, bf16[128,2048]{1,0:T(8,128)(2,1)}, u32[]{:S(2)}, u32[]{:S(2)}) collective-permute-start(bf16[128,2048]{1,0:T(8,128)(2,1)} %get-tuple-element.94), channel_id=1, source_target_pairs={{4,0},{8,4},{12,8},{5,1},{9,5},{13,9},{6,2},{10,6},{14,10},{7,3},{... | collective-permute-start | bytes 1572872 | tf_op jit(solution)/shard_map/ppermute | solution.py:37
  99.4 45.0 %collective-permute-start.12 = (bf16[1024,256]{1,0:T(8,128)(2,1)}, bf16[1024,256]{1,0:T(8,128)(2,1)}, u32[]{:S(2)}, u32[]{:S(2)}) collective-permute-start(bf16[1024,256]{1,0:T(8,128)(2,1)} %constant_dynamic-update-slice_fusion.8), channel_id=1, source_target_pairs={{0,4},{4,0},{8,12},{12,8},{1,5},{5,1},{9,13},{13,9},{2,6},{6,2},{1... | collective-permute-start | bytes 1572872 | tf_op jit(solution)/shard_map/ppermute | solution.py:76
  101.3 44.5 %collective-permute-start.13 = (bf16[1024,256]{1,0:T(8,128)(2,1)}, bf16[1024,256]{1,0:T(8,128)(2,1)}, u32[]{:S(2)}, u32[]{:S(2)}) collective-permute-start(bf16[1024,256]{1,0:T(8,128)(2,1)} %collective-permute-done.11), channel_id=1, source_target_pairs={{0,4},{4,0},{8,12},{12,8},{1,5},{5,1},{9,13},{13,9},{2,6},{6,2},{1... | collective-permute-start | bytes 1572872 | tf_op jit(solution)/shard_map/ppermute | solution.py:76
  125.8 26.0 %collective-permute-start.18 = (bf16[1024,768]{1,0:T(8,128)(2,1)}, bf16[1024,768]{1,0:T(8,128)(2,1)}, u32[]{:S(2)}, u32[]{:S(2)}) collective-permute-start(bf16[1024,768]{1,0:T(8,128)(2,1)} %constant_dynamic-update-slice_fusion.4), channel_id=1, source_target_pairs={{0,4},{4,0},{8,12},{12,8},{1,5},{5,1},{9,13},{13,9},{2,6},{6,2},{1... | collective-permute-start | bytes 4718600 | tf_op jit(solution)/shard_map/ppermute | solution.py:76
  125.8 28.0 %collective-permute-start.19 = (bf16[1024,768]{1,0:T(8,128)(2,1)}, bf16[1024,768]{1,0:T(8,128)(2,1)}, u32[]{:S(2)}, u32[]{:S(2)}) collective-permute-start(bf16[1024,768]{1,0:T(8,128)(2,1)} %collective-permute-done.17), channel_id=1, source_target_pairs={{0,4},{4,0},{8,12},{12,8},{1,5},{5,1},{9,13},{13,9},{2,6},{6,2},{1... | collective-permute-start | bytes 4718600 | tf_op jit(solution)/shard_map/ppermute | solution.py:76
  129.1 2.4 copy-start.1
  147.5 6.4 %copy-start.3 = (bf16[256,1024]{1,0:T(8,128)(2,1)}, bf16[256,1024]{1,0:T(8,128)(2,1)S(1)}, u32[]{:S(2)}) copy-start(bf16[256,1024]{1,0:T(8,128)(2,1)S(1)} %get-tuple-element.82) | copy-start | bytes 1572868
  158.6 41.3 %copy-start.7 = (bf16[2,128]{1,0:T(2,128)(2,1)S(1)}, bf16[2,128]{1,0:T(2,128)(2,1)}, u32[]{:S(2)}) copy-start(bf16[2,128]{1,0:T(2,128)(2,1)} %get-tuple-element.100) | copy-start | bytes 1540
  158.6 41.3 %all-to-all-start.1 = ((bf16[4,8,128,192]{2,3,1,0:T(8,128)(2,1)}), bf16[4,8,128,192]{2,3,1,0:T(8,128)(2,1)S(1)}, u32[]{:S(2)}, u32[]{:S(2)}) async-start(bf16[4,8,128,192]{2,3,1,0:T(8,128)(2,1)} %bitcast.26), calls=%async_computation.1 | async-start | bytes 3145728 | tf_op jit(solution)/shard_map/all_to_all | solution.py:189
  165.7 42.9 %collective-permute-start.20 = (bf16[256,256]{1,0:T(8,128)(2,1)S(1)}, bf16[256,256]{1,0:T(8,128)(2,1)S(1)}, u32[]{:S(2)}, u32[]{:S(2)}) collective-permute-start(bf16[256,256]{1,0:T(8,128)(2,1)S(1)} %get-tuple-element.90), channel_id=1, source_target_pairs={{0,1},{1,2},{2,3},{3,0},{4,5},{5,6},{6,7},{7,4},{8,9},{9,10},{10,1... | collective-permute-start | bytes 393224 | tf_op jit(solution)/shard_map/ppermute | solution.py:22
  200.5 12.6 %all-to-all-start = ((bf16[4,8,128]{2,1,0:T(8,128)(2,1)}), bf16[4,8,128]{2,1,0:T(8,128)(2,1)S(1)}, u32[]{:S(2)}, u32[]{:S(2)}) async-start(bf16[4,8,128]{2,1,0:T(8,128)(2,1)} %broadcast_in_dim.86), calls=%async_computation | async-start | bytes 16384 | tf_op jit(solution)/shard_map/all_to_all | solution.py:190
  208.5 30.4 %collective-permute-start.21 = (bf16[256,256]{1,0:T(8,128)(2,1)S(1)}, bf16[256,256]{1,0:T(8,128)(2,1)S(1)}, u32[]{:S(2)}, u32[]{:S(2)}) collective-permute-start(bf16[256,256]{1,0:T(8,128)(2,1)S(1)} %get-tuple-element.90), channel_id=1, source_target_pairs={{0,3},{1,0},{2,1},{3,2},{4,7},{5,4},{6,5},{7,6},{8,11},{9,8},{10,9... | collective-permute-start | bytes 393224 | tf_op jit(solution)/shard_map/ppermute | solution.py:27
  208.6 30.3 %collective-permute-start.22 = (bf16[256,256]{1,0:T(8,128)(2,1)S(1)}, bf16[256,256]{1,0:T(8,128)(2,1)S(1)}, u32[]{:S(2)}, u32[]{:S(2)}) collective-permute-start(bf16[256,256]{1,0:T(8,128)(2,1)S(1)} %collective-permute-done.20), channel_id=1, source_target_pairs={{0,1},{1,2},{2,3},{3,0},{4,5},{5,6},{6,7},{7,4},{8,9},{9,10},{10,1... | collective-permute-start | bytes 393224 | tf_op jit(solution)/shard_map/ppermute | solution.py:22
  230.4 10.2 %copy-start.6 = (s32[2,128]{1,0:T(2,128)S(1)}, s32[2,128]{1,0:T(2,128)}, u32[]{:S(2)}) copy-start(s32[2,128]{1,0:T(2,128)} %param.12) | copy-start | bytes 3076
  230.4 10.3 %copy-start.9 = (u32[32]{0:T(128)S(1)}, u32[32]{0:T(128)}, u32[]{:S(2)}) copy-start(u32[32]{0:T(128)} %constant.159) | copy-start | bytes 388
  232.0 40.8 %all-to-all-start.2 = ((bf16[4,2,32768]{2,1,0:T(2,128)(2,1)}), bf16[4,2,32768]{2,1,0:T(2,128)(2,1)S(1)}, u32[]{:S(2)}, u32[]{:S(2)}) async-start(bf16[4,2,32768]{2,1,0:T(2,128)(2,1)} %reshape.161), calls=%async_computation.2 | async-start | bytes 1048576 | tf_op jit(solution)/shard_map/all_to_all | solution.py:193
  238.9 130.1 %all-reduce.4.cloned.1.call-start = ((), (), s32[]{:S(2)}) async-start(), calls=%async_computation.3 | async-start | bytes 262144
  239.0 33.8 %collective-permute-start.23 = (bf16[1024,256]{1,0:T(8,128)(2,1)S(1)}, bf16[1024,256]{1,0:T(8,128)(2,1)S(1)}, u32[]{:S(2)}, u32[]{:S(2)}) collective-permute-start(bf16[1024,256]{1,0:T(8,128)(2,1)S(1)} %constant_dynamic-update-slice_fusion), channel_id=1, source_target_pairs={{0,16},{16,0},{1,17},{17,1},{2,18},{18,2},{3,19},{19,3},{4,20},{20... | collective-permute-start | bytes 1572872 | tf_op jit(solution)/shard_map/ppermute | solution.py:71
  240.6 35.3 %collective-permute-start.24 = (bf16[1024,256]{1,0:T(8,128)(2,1)S(1)}, bf16[1024,256]{1,0:T(8,128)(2,1)S(1)}, u32[]{:S(2)}, u32[]{:S(2)}) collective-permute-start(bf16[1024,256]{1,0:T(8,128)(2,1)S(1)} %constant_dynamic-update-slice_fusion), channel_id=1, source_target_pairs={{0,4},{4,0},{8,12},{12,8},{1,5},{5,1},{9,13},{13,9},{2,6},{6,2},{1... | collective-permute-start | bytes 1572872 | tf_op jit(solution)/shard_map/ppermute | solution.py:76
  272.8 3.5 collective-permute-start.25
  275.9 1.8 copy-start.4
  277.9 92.5 %copy-start.2 = (bf16[256,1024]{1,0:T(8,128)(2,1)}, bf16[256,1024]{1,0:T(8,128)(2,1)S(1)}, u32[]{:S(2)}) copy-start(bf16[256,1024]{1,0:T(8,128)(2,1)S(1)} %fusion.24) | copy-start | bytes 1572868
Sparse Core Ops, SparseCore 0:
  278.9 90.0 all-reduce.3
